TPU v7x, 512 devices: a whole 4x8x8 slice. The times are simulated.
512 devices in a mesh: rows: 32 (over y, x), vocab: 16 (over z, core).
Axes of the slice: x: 4, y: 8, z: 8, core: 2. Of those that a mesh axis runs over, the one named last changes fastest.
Arguments:
- hidden: bfloat16 [12288, 8192], P('rows', 'vocab'), may hold values from -128 to 128
- head: bfloat16 [8192, 8192], P('rows', 'vocab'), may hold values from -4 to 4
- targets: int32 [12288], P('rows'), may hold values from 0 to 128255
- live: int32 [12288], P('rows'), may hold values from 0 to 1, as said below
- prior_lse: float32 [12288], P('rows'), may hold values from 10 to 18
- prior_mean: float32 [12288], P('rows'), may hold values from 2 to 8
- prior_target: float32 [12288], P('rows'), may hold values from -12 to 12
- seq_lengths: int32 [32], replicated, may hold values from 1 to 768, 12288 in all
Outputs:
- logprob: float32 [12288], P(('rows', 'vocab'))
- entropy: float32 [12288], P(('rows', 'vocab'))
- seq_score: float32 [32], replicated
Inputs may be any that keep to these rules, and one draw needn't show every extreme that they name: Within the 384 rows of each index of rows, the live rows come first; every such index has at least 48 live rows and some index has all 384.
All inputs are finite; a program needn't handle non-finite values.
Results may differ from a plain program's by a relative error of at most 0.0003.
Values may be sent and summed in bfloat16 or wider, within the bound.
No kernel may reach another device: no remote copies, remote signals or barrier semaphores. Data moves between devices by JAX's collectives and lax.ppermute only.
A program may use at most 64 MiB of HBM per device.

v0:
```python
import jax
import jax.numpy as jnp
from jax import lax
from jax.sharding import PartitionSpec as P

VOCAB = 128256
SEQS = 32
GSIZE = 8


def finish_rows(block_peak, block_mass, block_moment, block_target, live, prior_lse, prior_mean):
    highest = jnp.maximum(block_peak, prior_lse)
    earlier = jnp.exp(prior_lse - highest)
    scaled = jnp.exp(block_peak - highest)
    total_mass = earlier + block_mass * scaled
    norm_log = highest + jnp.log(total_mass)
    average = (earlier * prior_mean + scaled * block_moment) / total_mass
    keeping = live.astype(jnp.float32)
    return (keeping * (block_target - norm_log), keeping * (norm_log - average))


def local(hidden, head, targets, live, prior_lse, prior_mean, prior_target, seq_lengths):
    rows_here = hidden.shape[0]
    cols_here = head.shape[1]
    spread = lax.axis_size("vocab")
    which = lax.axis_index("vocab")
    block_first = VOCAB - cols_here * spread
    first_col = block_first + which * cols_here
    gathered = lax.all_gather(hidden, "vocab", axis=1, tiled=True)
    logits = jnp.dot(
        gathered,
        lax.all_gather(head, "rows", axis=0, tiled=True),
        preferred_element_type=jnp.float32,
    )
    row_peak = jnp.max(logits, axis=1)
    weights = jnp.exp(logits - row_peak[:, None])
    row_mass = jnp.sum(weights, axis=1)
    moment = jnp.sum(weights * logits, axis=1)
    column = targets - first_col
    columns = lax.broadcasted_iota(jnp.int32, logits.shape, 1)
    picked = jnp.sum(jnp.where(columns == column[:, None], logits, jnp.zeros_like(logits)), axis=1)
    share = rows_here // spread
    begin = which * share

    def own_rows(values):
        return lax.dynamic_slice_in_dim(values, begin, share, 0)

    highest = lax.pmax(row_peak, "vocab")
    factor = jnp.exp(row_peak - highest)
    mass_all, moment_all, picked_all = lax.psum(
        (row_mass * factor, moment * factor, picked), "vocab"
    )
    peak_share = own_rows(highest)
    mass_share = own_rows(mass_all)
    moment_share = own_rows(moment_all)
    picked_share = own_rows(picked_all)
    target_share = own_rows(targets)
    block_target = jnp.where(target_share >= block_first, picked_share, own_rows(prior_target))
    logprob, entropy = finish_rows(
        peak_share,
        mass_share,
        moment_share,
        block_target,
        own_rows(live),
        own_rows(prior_lse),
        own_rows(prior_mean),
    )
    global_rows = lax.axis_index("rows") * rows_here + begin + jnp.arange(share, dtype=jnp.int32)
    endings = jnp.cumsum(seq_lengths)
    member = jnp.sum((global_rows[:, None] >= endings[None, :]).astype(jnp.int32), axis=1)
    onehot = (member[:, None] == jnp.arange(SEQS, dtype=jnp.int32)[None, :]).astype(jnp.float32)
    partial_sums = jnp.sum(onehot * logprob[:, None], axis=0)
    sums = lax.psum(partial_sums, ("rows", "vocab"))
    seq_mean = sums / seq_lengths.astype(jnp.float32)
    grouped = seq_mean.reshape(SEQS // GSIZE, GSIZE)
    seq_score = (grouped - jnp.mean(grouped, axis=1, keepdims=True)).reshape(SEQS)
    return (logprob, entropy, seq_score)


def solution(mesh):
    return jax.shard_map(
        local,
        mesh=mesh,
        in_specs=(
            P("rows", "vocab"),
            P("rows", "vocab"),
            P("rows"),
            P("rows"),
            P("rows"),
            P("rows"),
            P("rows"),
            P(),
        ),
        out_specs=(P(("rows", "vocab")), P(("rows", "vocab")), P()),
        check_vma=False,
    )
```

profile of v0, /device:TPU:1, one launch (start us, length us, event | category | flops | bytes accessed | tf_op | source)
XLA Modules:
  0.0 332.5 jit_solution(5648980550424565232)
XLA Ops:
  7.2 0.0 all-gather.3.cloned.1.call-start
  7.2 0.7 all-gather.3.cloned.1.call-update
  7.9 0.0 all-gather.5.cloned.1.call-start
  7.9 0.7 all-gather.5.cloned.1.call-update
  8.7 0.7 copy.13
  9.4 0.1 reduce-window.8
  9.4 0.1 reduce
  9.6 0.2 convert_reduce_fusion
  9.8 0.7 broadcast_subtract_fusion
  10.4 0.0 copy-start
  10.4 55.1 %all-gather.3.cloned.1.call-done = bf16[384,8192]{1,0:T(8,128)(2,1)} async-done(((bf16[384,512]{1,0:T(8,128)(2,1)}), bf16[384,8192]{1,0:T(8,128)(2,1)}) %all-gather.3.cloned.1.call-update) | async-done | bytes 6291472 | tf_op jit(solution)/shard_map/all_gather | solution.py:29
  65.6 103.9 %all-gather.5.cloned.1.call-done = bf16[8192,512]{1,0:T(8,128)(2,1)} async-done(((bf16[256,512]{1,0:T(8,128)(2,1)}), bf16[8192,512]{1,0:T(8,128)(2,1)}) %all-gather.5.cloned.1.call-update) | async-done | bytes 8388624 | tf_op jit(solution)/shard_map/all_gather | solution.py:32
  169.4 8.0 %fusion.5 = (f32[384]{0:T(512)S(1)}, f32[384,512]{1,0:T(8,128)S(1)}) fusion(bf16[384,8192]{1,0:T(8,128)(2,1)} %all-gather.3.cloned.1.call-done, bf16[8192,512]{1,0:T(8,128)(2,1)} %all-gather.5.cloned.1.call-done), kind=kOutput, calls=%fused_computation.24 | convolution fusion | flops 3221421568 | bytes 15468032 | tf_op jit(solution)/shard_map/dot_general | solution.py:30
  177.4 25.1 %pmax.7 = f32[384]{0:T(512)S(1)} all-reduce(f32[384]{0:T(512)S(1)} %get-tuple-element.13), channel_id=1, replica_groups=mesh['rows'=32,'vocab'=16] {'vocab'}, use_global_device_ids=true, to_apply=%region_3.4 | all-reduce | flops 384 | bytes 3072 | tf_op jit(solution)/shard_map/pmax | solution.py:48
  202.5 0.5 multiply_reduce_fusion
  203.0 25.8 %all-reduce = (f32[384]{0:T(512)S(1)}, f32[384]{0:T(512)S(1)}, f32[384]{0:T(512)S(1)}) all-reduce(f32[384]{0:T(512)S(1)} %get-tuple-element.5, f32[384]{0:T(512)S(1)} %get-tuple-element.12, f32[384]{0:T(512)S(1)} %get-tuple-element.11), channel_id=1, replica_groups=mesh['rows'=32,'vocab'=16] {'vocab'}, use_global_device_ids=true, to_apply=%region_1.0 | all-reduce | flops 1152 | bytes 9216 | tf_op jit(solution)/shard_map/psum | solution.py:50
  228.9 1.4 subtract_multiply_fusion
  230.2 0.0 copy-start.1
  230.2 0.1 select_reduce_fusion.1
  230.3 94.4 %psum.31 = f32[32]{0:T(128)S(1)} all-reduce(f32[32]{0:T(128)S(1)} %select_reduce_fusion.1), channel_id=1, replica_groups=mesh['rows'=32,'vocab'=16] {'rows','vocab'}, use_global_device_ids=true, to_apply=%region_11.12 | all-reduce | flops 32 | bytes 256 | tf_op jit(solution)/shard_map/psum | solution.py:73
  324.7 0.0 copy-done
  324.7 0.1 reshape.49
  324.8 0.1 reduce_sum.59
  325.0 0.1 sub.49
  325.0 0.1 sub.50
  325.1 0.5 sub.51
  325.6 0.0 copy-done.1
  (4 shorter events, 0.0 us)
Async XLA Ops:
  7.2 58.4 %all-gather.3.cloned.1.call-start = ((), (), s32[]{:S(2)}) async-start(), calls=%async_computation | async-start | bytes 6684672 | tf_op jit(solution)/shard_map/all_gather | solution.py:29
  7.9 161.5 %all-gather.5.cloned.1.call-start = ((), (), s32[]{:S(2)}) async-start(), calls=%async_computation.1 | async-start | bytes 8650752 | tf_op jit(solution)/shard_map/all_gather | solution.py:32
  10.4 314.3 %copy-start = (s32[32]{0:T(128)S(1)}, s32[32]{0:T(128)}, u32[]{:S(2)}) copy-start(s32[32]{0:T(128)} %param.15) | copy-start | bytes 388
  230.2 95.4 %copy-start.1 = (f32[24]{0:T(128)}, f32[24]{0:T(128)S(1)}, u32[]{:S(2)}) copy-start(f32[24]{0:T(128)S(1)} %get-tuple-element.10) | copy-start | bytes 292
Sparse Core Ops, SparseCore 0:
  10.1 55.3 all-gather.2
  68.7 100.6 all-gather.4
where the time goes:
time: 333 us; the launch traced here: 332 us
  waiting for transfers between devices  160 us (48%)
  blocking collectives  145 us (44%)
  between operations  14.1 us (4%)
  matrix products  8 us (2%)
  other arithmetic  3.64 us (1%)
    all_gather x1, waiting for transfers between devices, local(): lax.all_gather(head, 'rows', axis=0, tiled=True)  104 us
    psum x1, blocking collectives, local(): sums = lax.psum(partial_sums, ('rows', 'vocab'))  94.4 us
    all_gather x1, waiting for transfers between devices, local(): gathered = lax.all_gather(hidden, 'vocab', axis=1, tiled=True)  55.1 us
    psum x1, blocking collectives, local(): lax.psum((row_mass * factor, moment * factor, picked), 'vocab')  25.8 us
    pmax x1, blocking collectives, local(): highest = lax.pmax(row_peak, 'vocab')  25.1 us
    dot_general x1, matrix products, local(): jnp.dot(gathered, lax.all_gather(head, 'rows', axis=0, tiled=True), prefe...  8 us
  transfers between devices with their start and end apart: 2, of which 2 were waited for; matrix products, arithmetic and copies ran while one was open for 1% of the time, Pallas kernels for 0%

commit v1 on v0

--- a/solution.py
+++ b/solution.py
@@ -6,6 +6,27 @@
 VOCAB = 128256
 SEQS = 32
 GSIZE = 8
+
+
+def gather_around(x, axis, dim):
+    size, place, width = (lax.axis_size(axis), lax.axis_index(axis), x.shape[dim])
+    right = [(i, (i + 1) % size) for i in range(size)]
+    left = [(i, (i - 1) % size) for i in range(size)]
+    result = jnp.zeros((*x.shape[:dim], size * width, *x.shape[dim + 1 :]), x.dtype)
+    result = lax.dynamic_update_slice_in_dim(result, x, place * width, axis=dim)
+    from_left = from_right = x
+    middle = size // 2
+    for turn in range(1, middle + 1):
+        from_left = lax.ppermute(from_left, axis, right)
+        result = lax.dynamic_update_slice_in_dim(
+            result, from_left, (place - turn) % size * width, axis=dim
+        )
+        if turn < size - middle:
+            from_right = lax.ppermute(from_right, axis, left)
+            result = lax.dynamic_update_slice_in_dim(
+                result, from_right, (place + turn) % size * width, axis=dim
+            )
+    return result
 
 
 def finish_rows(block_peak, block_mass, block_moment, block_target, live, prior_lse, prior_mean):
@@ -26,7 +47,7 @@
     which = lax.axis_index("vocab")
     block_first = VOCAB - cols_here * spread
     first_col = block_first + which * cols_here
-    gathered = lax.all_gather(hidden, "vocab", axis=1, tiled=True)
+    gathered = gather_around(hidden, "vocab", 1)
     logits = jnp.dot(
         gathered,
         lax.all_gather(head, "rows", axis=0, tiled=True),

time: 333 us -> 283 us (0.85)
  waiting for transfers between devices: 160 us -> 48.6 us
  starting transfers between devices: 0.08 us -> 40.5 us
  local copies, waits for them, and re-layouts: 0.99 us -> 19.1 us
    all_gather x1, waiting for transfers between devices: 104 us -> 41.5 us  [local(): lax.all_gather(head, 'rows', axis=0, tiled=True)]
    all_gather x1 -> x0, waiting for transfers between devices: 55.1 us -> none  [local(): gathered = lax.all_gather(hidden, 'vocab', axis=1, tiled=True)]
    ppermute x0 -> x15, starting transfers between devices: none -> 40.5 us  [the longest x7 33.4 us: gather_around(): from_right = lax.ppermute(from_right, axis, left)]
    dynamic_update_slice x0 -> x16, local copies, waits for them, and re-layouts: none -> 14.1 us  [the longest x8 7.45 us: gather_around(): lax.dynamic_update_slice_in_dim(result, from_left, (place - turn) % size...]
    ppermute x0 -> x15, waiting for transfers between devices: none -> 6.41 us  [the longest x8 5.45 us: gather_around(): from_left = lax.ppermute(from_left, axis, right)]
    broadcast_in_dim x0 -> x1, local copies, waits for them, and re-layouts: none -> 3.46 us  [gather_around(): jnp.zeros((*x.shape[:dim], size * width, *x.shape[dim + 1:]), x.dtype)]
  transfers between devices with their start and end apart: 2 -> 16, of which waited for: 2 -> 9; matrix products, arithmetic and copies ran while one was open for 1% -> 8% of each run, Pallas kernels for 0% -> 0%
where the time goes in v1:
time: 283 us
  blocking collectives  145 us (51%)
  waiting for transfers between devices  48.6 us (17%)
  starting transfers between devices  40.5 us (14%)
  local copies, waits for them, and re-layouts  19.1 us (7%)
  between operations  14.4 us (5%)
  matrix products  8 us (3%)
  other arithmetic  6.64 us (2%)
    psum x1, blocking collectives, local(): sums = lax.psum(partial_sums, ('rows', 'vocab'))  94.4 us
    all_gather x1, waiting for transfers between devices, local(): lax.all_gather(head, 'rows', axis=0, tiled=True)  41.5 us
    ppermute x7, starting transfers between devices, gather_around(): from_right = lax.ppermute(from_right, axis, left)  33.4 us
    psum x1, blocking collectives, local(): lax.psum((row_mass * factor, moment * factor, picked), 'vocab')  25.8 us
    pmax x1, blocking collectives, local(): highest = lax.pmax(row_peak, 'vocab')  25.1 us
    dot_general x1, matrix products, local(): jnp.dot(gathered, lax.all_gather(head, 'rows', axis=0, tiled=True), prefe...  8 us
    dynamic_update_slice x8, local copies, waits for them, and re-layouts, gather_around(): lax.dynamic_update_slice_in_dim(result, from_left, (place - turn) % size...  7.45 us
    ppermute x8, starting transfers between devices, gather_around(): from_left = lax.ppermute(from_left, axis, right)  7.12 us
  transfers between devices with their start and end apart: 16, of which 9 were waited for; matrix products, arithmetic and copies ran while one was open for 8% of the time, Pallas kernels for 0%

profile of v1, /device:TPU:1, one launch (start us, length us, event | category | flops | bytes accessed | tf_op | source)
XLA Modules:
  0.0 282.7 jit_solution(294875742223112869)
XLA Ops:
  7.2 0.7 all-gather.2.cloned.1.call-update
  7.9 3.5 %collective-permute-start = (bf16[384,512]{1,0:T(8,128)(2,1)}, bf16[384,512]{1,0:T(8,128)(2,1)S(1)}, u32[]{:S(2)}, u32[]{:S(2)}) collective-permute-start(bf16[384,512]{1,0:T(8,128)(2,1)} %param.8), channel_id=1, source_target_pairs={{0,1},{1,2},{2,3},{3,4},{4,5},{5,6},{6,7},{7,8},{8,9},{9,10},{10,1... | collective-permute-start | bytes 1179656 | tf_op jit(solution)/shard_map/ppermute | solution.py:20
  11.4 3.4 %collective-permute-start.1 = (bf16[384,512]{1,0:T(8,128)(2,1)}, bf16[384,512]{1,0:T(8,128)(2,1)S(1)}, u32[]{:S(2)}, u32[]{:S(2)}) collective-permute-start(bf16[384,512]{1,0:T(8,128)(2,1)} %param.8), channel_id=1, source_target_pairs={{0,15},{1,0},{2,1},{3,2},{4,3},{5,4},{6,5},{7,6},{8,7},{9,8},{10,9... | collective-permute-start | bytes 1179656 | tf_op jit(solution)/shard_map/ppermute | solution.py:25
  14.8 1.6 collective-permute-done
  16.4 2.4 collective-permute-start.2
  18.8 0.3 collective-permute-done.1
  19.1 4.5 %collective-permute-start.3 = (bf16[384,512]{1,0:T(8,128)(2,1)S(1)}, bf16[384,512]{1,0:T(8,128)(2,1)S(1)}, u32[]{:S(2)}, u32[]{:S(2)}) collective-permute-start(bf16[384,512]{1,0:T(8,128)(2,1)S(1)} %collective-permute-done.1), channel_id=1, source_target_pairs={{0,15},{1,0},{2,1},{3,2},{4,3},{5,4},{6,5},{7,6},{8,7},{9,8},{10,9... | collective-permute-start | bytes 1179656 | tf_op jit(solution)/shard_map/ppermute | solution.py:25
  23.6 1.2 collective-permute-done.2
  24.8 1.2 collective-permute-start.4
  26.0 0.3 collective-permute-done.3
  26.3 5.7 %collective-permute-start.5 = (bf16[384,512]{1,0:T(8,128)(2,1)S(1)}, bf16[384,512]{1,0:T(8,128)(2,1)S(1)}, u32[]{:S(2)}, u32[]{:S(2)}) collective-permute-start(bf16[384,512]{1,0:T(8,128)(2,1)S(1)} %collective-permute-done.3), channel_id=1, source_target_pairs={{0,15},{1,0},{2,1},{3,2},{4,3},{5,4},{6,5},{7,6},{8,7},{9,8},{10,9... | collective-permute-start | bytes 1179656 | tf_op jit(solution)/shard_map/ppermute | solution.py:25
  32.0 1.2 collective-permute-done.4
  33.2 1.3 broadcast_subtract_fusion
  34.5 7.2 %collective-permute-start.7 = (bf16[384,512]{1,0:T(8,128)(2,1)S(1)}, bf16[384,512]{1,0:T(8,128)(2,1)S(1)}, u32[]{:S(2)}, u32[]{:S(2)}) collective-permute-start(bf16[384,512]{1,0:T(8,128)(2,1)S(1)} %collective-permute-done.5), channel_id=1, source_target_pairs={{0,15},{1,0},{2,1},{3,2},{4,3},{5,4},{6,5},{7,6},{8,7},{9,8},{10,9... | collective-permute-start | bytes 1179656 | tf_op jit(solution)/shard_map/ppermute | solution.py:25
  41.7 0.5 iota_add_fusion
  42.2 1.3 copy.13
  43.5 0.8 reduce-window.8
  44.3 0.6 reduce
  44.9 0.9 convert_reduce_fusion
  46.1 3.5 %broadcast_in_dim.4 = bf16[384,8192]{1,0:T(8,128)(2,1)} broadcast(bf16[]{:T(256)} %constant.111.clone.1), dimensions={} | broadcast | bytes 6291458 | tf_op jit(solution)/shard_map/broadcast_in_dim | solution.py:15
  49.6 0.9 constant_dynamic-update-slice_fusion.15
  50.4 0.9 constant_dynamic-update-slice_fusion.14
  51.3 3.8 %collective-permute-start.9 = (bf16[384,512]{1,0:T(8,128)(2,1)S(1)}, bf16[384,512]{1,0:T(8,128)(2,1)S(1)}, u32[]{:S(2)}, u32[]{:S(2)}) collective-permute-start(bf16[384,512]{1,0:T(8,128)(2,1)S(1)} %collective-permute-done.7), channel_id=1, source_target_pairs={{0,15},{1,0},{2,1},{3,2},{4,3},{5,4},{6,5},{7,6},{8,7},{9,8},{10,9... | collective-permute-start | bytes 1179656 | tf_op jit(solution)/shard_map/ppermute | solution.py:25
  55.1 0.8 constant_dynamic-update-slice_fusion.13
  56.0 0.8 constant_dynamic-update-slice_fusion.12
  56.8 0.8 constant_dynamic-update-slice_fusion.11
  57.6 0.8 constant_dynamic-update-slice_fusion.10
  58.6 4.6 %collective-permute-start.11 = (bf16[384,512]{1,0:T(8,128)(2,1)S(1)}, bf16[384,512]{1,0:T(8,128)(2,1)S(1)}, u32[]{:S(2)}, u32[]{:S(2)}) collective-permute-start(bf16[384,512]{1,0:T(8,128)(2,1)S(1)} %collective-permute-done.9), channel_id=1, source_target_pairs={{0,15},{1,0},{2,1},{3,2},{4,3},{5,4},{6,5},{7,6},{8,7},{9,8},{10,9... | collective-permute-start | bytes 1179656 | tf_op jit(solution)/shard_map/ppermute | solution.py:25
  63.3 0.8 constant_dynamic-update-slice_fusion.9
  64.1 0.8 constant_dynamic-update-slice_fusion.8
  64.9 0.8 constant_dynamic-update-slice_fusion.7
  65.7 1.8 constant_dynamic-update-slice_fusion.6
  67.5 4.2 %collective-permute-start.13 = (bf16[384,512]{1,0:T(8,128)(2,1)S(1)}, bf16[384,512]{1,0:T(8,128)(2,1)S(1)}, u32[]{:S(2)}, u32[]{:S(2)}) collective-permute-start(bf16[384,512]{1,0:T(8,128)(2,1)S(1)} %collective-permute-done.11), channel_id=1, source_target_pairs={{0,15},{1,0},{2,1},{3,2},{4,3},{5,4},{6,5},{7,6},{8,7},{9,8},{10,9... | collective-permute-start | bytes 1179656 | tf_op jit(solution)/shard_map/ppermute | solution.py:25
  71.7 0.8 constant_dynamic-update-slice_fusion.5
  72.5 0.8 constant_dynamic-update-slice_fusion.4
  73.3 0.8 constant_dynamic-update-slice_fusion.3
  74.1 0.8 constant_dynamic-update-slice_fusion.2
  75.0 0.8 constant_dynamic-update-slice_fusion.1
  75.8 1.4 collective-permute-done.14
  77.2 0.8 constant_dynamic-update-slice_fusion
  78.0 41.5 %all-gather.2.cloned.1.call-done = bf16[8192,512]{1,0:T(8,128)(2,1)} async-done(((bf16[256,512]{1,0:T(8,128)(2,1)}), bf16[8192,512]{1,0:T(8,128)(2,1)}) %all-gather.2.cloned.1.call-update) | async-done | bytes 8388624 | tf_op jit(solution)/shard_map/all_gather | solution.py:53
  119.6 8.0 %fusion.5 = (f32[384]{0:T(512)S(1)}, f32[384,512]{1,0:T(8,128)S(1)}) fusion(bf16[384,8192]{1,0:T(8,128)(2,1)} %constant_dynamic-update-slice_fusion, bf16[8192,512]{1,0:T(8,128)(2,1)} %all-gather.2.cloned.1.call-done), kind=kOutput, calls=%fused_computation.40 | convolution fusion | flops 3221421568 | bytes 15468032 | tf_op jit(solution)/shard_map/dot_general | solution.py:51
  127.6 25.1 %pmax.7 = f32[384]{0:T(512)S(1)} all-reduce(f32[384]{0:T(512)S(1)} %get-tuple-element.13), channel_id=1, replica_groups=mesh['rows'=32,'vocab'=16] {'vocab'}, use_global_device_ids=true, to_apply=%region_3.4 | all-reduce | flops 384 | bytes 3072 | tf_op jit(solution)/shard_map/pmax | solution.py:69
  152.7 0.5 multiply_reduce_fusion
  153.2 25.8 %all-reduce = (f32[384]{0:T(512)S(1)}, f32[384]{0:T(512)S(1)}, f32[384]{0:T(512)S(1)}) all-reduce(f32[384]{0:T(512)S(1)} %get-tuple-element.5, f32[384]{0:T(512)S(1)} %get-tuple-element.12, f32[384]{0:T(512)S(1)} %get-tuple-element.11), channel_id=1, replica_groups=mesh['rows'=32,'vocab'=16] {'vocab'}, use_global_device_ids=true, to_apply=%region_1.2 | all-reduce | flops 1152 | bytes 9216 | tf_op jit(solution)/shard_map/psum | solution.py:71
  179.0 1.4 subtract_multiply_fusion
  180.5 94.4 %psum.31 = f32[32]{0:T(128)S(1)} all-reduce(f32[32]{0:T(128)S(1)} %select_reduce_fusion.1), channel_id=1, replica_groups=mesh['rows'=32,'vocab'=16] {'rows','vocab'}, use_global_device_ids=true, to_apply=%region_11.12 | all-reduce | flops 32 | bytes 256 | tf_op jit(solution)/shard_map/psum | solution.py:94
  275.3 0.5 sub.83
  (31 shorter events, 0.9 us)
Async XLA Ops:
  7.2 42.4 %copy-start = (bf16[384,512]{1,0:T(8,128)(2,1)S(1)}, bf16[384,512]{1,0:T(8,128)(2,1)}, u32[]{:S(2)}) copy-start(bf16[384,512]{1,0:T(8,128)(2,1)} %param.8) | copy-start | bytes 1179652
  7.2 112.4 %all-gather.2.cloned.1.call-start = ((), (), s32[]{:S(2)}) async-start(), calls=%async_computation | async-start | bytes 8650752 | tf_op jit(solution)/shard_map/all_gather | solution.py:53
  7.9 8.5 %collective-permute-start = (bf16[384,512]{1,0:T(8,128)(2,1)}, bf16[384,512]{1,0:T(8,128)(2,1)S(1)}, u32[]{:S(2)}, u32[]{:S(2)}) collective-permute-start(bf16[384,512]{1,0:T(8,128)(2,1)} %param.8), channel_id=1, source_target_pairs={{0,1},{1,2},{2,3},{3,4},{4,5},{5,6},{6,7},{7,8},{8,9},{9,10},{10,1... | collective-permute-start | bytes 1179656 | tf_op jit(solution)/shard_map/ppermute | solution.py:20
  11.4 7.7 %collective-permute-start.1 = (bf16[384,512]{1,0:T(8,128)(2,1)}, bf16[384,512]{1,0:T(8,128)(2,1)S(1)}, u32[]{:S(2)}, u32[]{:S(2)}) collective-permute-start(bf16[384,512]{1,0:T(8,128)(2,1)} %param.8), channel_id=1, source_target_pairs={{0,15},{1,0},{2,1},{3,2},{4,3},{5,4},{6,5},{7,6},{8,7},{9,8},{10,9... | collective-permute-start | bytes 1179656 | tf_op jit(solution)/shard_map/ppermute | solution.py:25
  16.4 8.4 %collective-permute-start.2 = (bf16[384,512]{1,0:T(8,128)(2,1)S(1)}, bf16[384,512]{1,0:T(8,128)(2,1)S(1)}, u32[]{:S(2)}, u32[]{:S(2)}) collective-permute-start(bf16[384,512]{1,0:T(8,128)(2,1)S(1)} %collective-permute-done), channel_id=1, source_target_pairs={{0,1},{1,2},{2,3},{3,4},{4,5},{5,6},{6,7},{7,8},{8,9},{9,10},{10,1... | collective-permute-start | bytes 1179656 | tf_op jit(solution)/shard_map/ppermute | solution.py:20
  19.1 7.2 %collective-permute-start.3 = (bf16[384,512]{1,0:T(8,128)(2,1)S(1)}, bf16[384,512]{1,0:T(8,128)(2,1)S(1)}, u32[]{:S(2)}, u32[]{:S(2)}) collective-permute-start(bf16[384,512]{1,0:T(8,128)(2,1)S(1)} %collective-permute-done.1), channel_id=1, source_target_pairs={{0,15},{1,0},{2,1},{3,2},{4,3},{5,4},{6,5},{7,6},{8,7},{9,8},{10,9... | collective-permute-start | bytes 1179656 | tf_op jit(solution)/shard_map/ppermute | solution.py:25
  24.8 8.4 %collective-permute-start.4 = (bf16[384,512]{1,0:T(8,128)(2,1)S(1)}, bf16[384,512]{1,0:T(8,128)(2,1)S(1)}, u32[]{:S(2)}, u32[]{:S(2)}) collective-permute-start(bf16[384,512]{1,0:T(8,128)(2,1)S(1)} %collective-permute-done.2), channel_id=1, source_target_pairs={{0,1},{1,2},{2,3},{3,4},{4,5},{5,6},{6,7},{7,8},{8,9},{9,10},{10,1... | collective-permute-start | bytes 1179656 | tf_op jit(solution)/shard_map/ppermute | solution.py:20
  26.3 8.2 %collective-permute-start.5 = (bf16[384,512]{1,0:T(8,128)(2,1)S(1)}, bf16[384,512]{1,0:T(8,128)(2,1)S(1)}, u32[]{:S(2)}, u32[]{:S(2)}) collective-permute-start(bf16[384,512]{1,0:T(8,128)(2,1)S(1)} %collective-permute-done.3), channel_id=1, source_target_pairs={{0,15},{1,0},{2,1},{3,2},{4,3},{5,4},{6,5},{7,6},{8,7},{9,8},{10,9... | collective-permute-start | bytes 1179656 | tf_op jit(solution)/shard_map/ppermute | solution.py:25
  33.2 11.7 %collective-permute-start.6 = (bf16[384,512]{1,0:T(8,128)(2,1)S(1)}, bf16[384,512]{1,0:T(8,128)(2,1)S(1)}, u32[]{:S(2)}, u32[]{:S(2)}) collective-permute-start(bf16[384,512]{1,0:T(8,128)(2,1)S(1)} %collective-permute-done.4), channel_id=1, source_target_pairs={{0,1},{1,2},{2,3},{3,4},{4,5},{5,6},{6,7},{7,8},{8,9},{9,10},{10,1... | collective-permute-start | bytes 1179656 | tf_op jit(solution)/shard_map/ppermute | solution.py:20
  34.5 16.8 %collective-permute-start.7 = (bf16[384,512]{1,0:T(8,128)(2,1)S(1)}, bf16[384,512]{1,0:T(8,128)(2,1)S(1)}, u32[]{:S(2)}, u32[]{:S(2)}) collective-permute-start(bf16[384,512]{1,0:T(8,128)(2,1)S(1)} %collective-permute-done.5), channel_id=1, source_target_pairs={{0,15},{1,0},{2,1},{3,2},{4,3},{5,4},{6,5},{7,6},{8,7},{9,8},{10,9... | collective-permute-start | bytes 1179656 | tf_op jit(solution)/shard_map/ppermute | solution.py:25
  44.9 11.0 %collective-permute-start.8 = (bf16[384,512]{1,0:T(8,128)(2,1)S(1)}, bf16[384,512]{1,0:T(8,128)(2,1)}, u32[]{:S(2)}, u32[]{:S(2)}) collective-permute-start(bf16[384,512]{1,0:T(8,128)(2,1)S(1)} %collective-permute-done.6), channel_id=1, source_target_pairs={{0,1},{1,2},{2,3},{3,4},{4,5},{5,6},{6,7},{7,8},{8,9},{9,10},{10,1... | collective-permute-start | bytes 1179656 | tf_op jit(solution)/shard_map/ppermute | solution.py:20
  51.3 7.3 %collective-permute-start.9 = (bf16[384,512]{1,0:T(8,128)(2,1)S(1)}, bf16[384,512]{1,0:T(8,128)(2,1)S(1)}, u32[]{:S(2)}, u32[]{:S(2)}) collective-permute-start(bf16[384,512]{1,0:T(8,128)(2,1)S(1)} %collective-permute-done.7), channel_id=1, source_target_pairs={{0,15},{1,0},{2,1},{3,2},{4,3},{5,4},{6,5},{7,6},{8,7},{9,8},{10,9... | collective-permute-start | bytes 1179656 | tf_op jit(solution)/shard_map/ppermute | solution.py:25
  56.0 8.1 %collective-permute-start.10 = (bf16[384,512]{1,0:T(8,128)(2,1)}, bf16[384,512]{1,0:T(8,128)(2,1)S(1)}, u32[]{:S(2)}, u32[]{:S(2)}) collective-permute-start(bf16[384,512]{1,0:T(8,128)(2,1)} %collective-permute-done.8), channel_id=1, source_target_pairs={{0,1},{1,2},{2,3},{3,4},{4,5},{5,6},{6,7},{7,8},{8,9},{9,10},{10,1... | collective-permute-start | bytes 1179656 | tf_op jit(solution)/shard_map/ppermute | solution.py:20
  58.6 8.9 %collective-permute-start.11 = (bf16[384,512]{1,0:T(8,128)(2,1)S(1)}, bf16[384,512]{1,0:T(8,128)(2,1)S(1)}, u32[]{:S(2)}, u32[]{:S(2)}) collective-permute-start(bf16[384,512]{1,0:T(8,128)(2,1)S(1)} %collective-permute-done.9), channel_id=1, source_target_pairs={{0,15},{1,0},{2,1},{3,2},{4,3},{5,4},{6,5},{7,6},{8,7},{9,8},{10,9... | collective-permute-start | bytes 1179656 | tf_op jit(solution)/shard_map/ppermute | solution.py:25
  64.1 8.4 %collective-permute-start.12 = (bf16[384,512]{1,0:T(8,128)(2,1)S(1)}, bf16[384,512]{1,0:T(8,128)(2,1)S(1)}, u32[]{:S(2)}, u32[]{:S(2)}) collective-permute-start(bf16[384,512]{1,0:T(8,128)(2,1)S(1)} %collective-permute-done.10), channel_id=1, source_target_pairs={{0,1},{1,2},{2,3},{3,4},{4,5},{5,6},{6,7},{7,8},{8,9},{9,10},{10,1... | collective-permute-start | bytes 1179656 | tf_op jit(solution)/shard_map/ppermute | solution.py:20
  67.5 7.5 %collective-permute-start.13 = (bf16[384,512]{1,0:T(8,128)(2,1)S(1)}, bf16[384,512]{1,0:T(8,128)(2,1)S(1)}, u32[]{:S(2)}, u32[]{:S(2)}) collective-permute-start(bf16[384,512]{1,0:T(8,128)(2,1)S(1)} %collective-permute-done.11), channel_id=1, source_target_pairs={{0,15},{1,0},{2,1},{3,2},{4,3},{5,4},{6,5},{7,6},{8,7},{9,8},{10,9... | collective-permute-start | bytes 1179656 | tf_op jit(solution)/shard_map/ppermute | solution.py:25
  72.5 4.7 %collective-permute-start.14 = (bf16[384,512]{1,0:T(8,128)(2,1)S(1)}, bf16[384,512]{1,0:T(8,128)(2,1)S(1)}, u32[]{:S(2)}, u32[]{:S(2)}) collective-permute-start(bf16[384,512]{1,0:T(8,128)(2,1)S(1)} %collective-permute-done.12), channel_id=1, source_target_pairs={{0,1},{1,2},{2,3},{3,4},{4,5},{5,6},{6,7},{7,8},{8,9},{9,10},{10,1... | collective-permute-start | bytes 1179656 | tf_op jit(solution)/shard_map/ppermute | solution.py:20
  78.0 74.7 %copy-start.1 = (s32[384]{0:T(512)S(1)}, s32[384]{0:T(512)}, u32[]{:S(2)}) copy-start(s32[384]{0:T(512)} %broadcast_subtract_fusion) | copy-start | bytes 4612
  78.0 196.9 %copy-start.2 = (s32[32]{0:T(128)S(1)}, s32[32]{0:T(128)}, u32[]{:S(2)}) copy-start(s32[32]{0:T(128)} %param.15) | copy-start | bytes 388
  180.4 95.4 %copy-start.3 = (f32[24]{0:T(128)}, f32[24]{0:T(128)S(1)}, u32[]{:S(2)}) copy-start(f32[24]{0:T(128)S(1)} %get-tuple-element.10) | copy-start | bytes 292
Sparse Core Ops, SparseCore 0:
  11.2 108.3 all-gather.1
